TPU v7x, 256 devices: a whole 4x4x8 slice. The times are simulated.
256 devices in a mesh: row: 32 (over y, x, core), col: 8 (over z).
Axes of the slice: x: 4, y: 4, z: 8, core: 2. Of those that a mesh axis runs over, the one named last changes fastest.
Arguments:
- covariance: float32 [8192, 8192], P('row', 'col'), may hold values from 0 to 4, as said below
- panels: int32 [4], replicated, may hold values from 0 to 31, as said below
- observed: float32 [8192], P('row'), may hold values from -6 to 6
- drift_basis: float32 [64, 8192], P(None, 'row'), may hold values from -1.5 to 1.5
Outputs:
- complement: float32 [8192, 8192], P('row', 'col')
- factor: float32 [8192, 1024], P('row')
- solved_data: float32 [8192], P('row')
- solved_drift: float32 [64, 8192], P(None, 'row')
Inputs may be any that keep to these rules, and one draw needn't show every extreme that they name: `covariance`: symmetric and positive definite. `panels`: 4 different tile indices; tile 32 - 1 is always among them.
All inputs are finite; a program needn't handle non-finite values.
Results may differ from a plain program's by a relative error of at most 0.0003.
Values sent between devices are 32-bit elements; how exact they have to be, the bound alone decides.
No kernel may reach another device: no remote copies, remote signals or barrier semaphores. Data moves between devices by JAX's collectives and lax.ppermute only.
A program may use at most 64 MiB of HBM per device.

v0:
```python
import jax
import jax.numpy as jnp
from jax import lax
from jax.sharding import PartitionSpec as P

B = 256
K = 4
HIGH = lax.Precision.HIGHEST


def keep_mask(tiles, chosen):
    return jnp.all(tiles[:, None] != chosen[None, :], axis=1).astype(jnp.float32)


def dot(a, b):
    return lax.dot_general(a, b, (((1,), (0,)), ((), ())), precision=HIGH)


def dot_nt(a, b):
    return lax.dot_general(a, b, (((1,), (1,)), ((), ())), precision=HIGH)


def panel_keep(tiles, panels):
    cols = []
    for p in range(K):
        cols.append(jnp.broadcast_to(keep_mask(tiles, panels[:p])[:, None], (tiles.shape[0], B)))
    return jnp.concatenate(cols, axis=1)


def on_device(covariance, panels, observed, drift_basis):
    rows_here = covariance.shape[0]
    cols_here = covariance.shape[1]
    r = lax.axis_index("row")
    row_start = r * rows_here
    col_start = lax.axis_index("col") * cols_here
    row_tiles = (row_start + lax.iota(jnp.int32, rows_here)) // B
    col_tiles = (col_start + lax.iota(jnp.int32, cols_here)) // B
    sides = jnp.concatenate([observed[None, :], drift_basis], axis=0)
    with jax.named_scope("gather_row_strip"):
        strip = lax.all_gather(covariance, "col", axis=1, tiled=True)
        panel_cols = jnp.concatenate(
            [lax.dynamic_slice_in_dim(strip, panels[j] * B, B, 1) for j in range(K)], axis=1
        )
    with jax.named_scope("share_panel_rows"):
        s_rows, a_rows, w_cols = ([], [], [])
        for j in range(K):
            off = panels[j] * B - row_start
            mine = (off >= 0) & (off < rows_here)
            off = jnp.clip(off, 0, rows_here - B)
            s_rows.append(jnp.where(mine, lax.dynamic_slice_in_dim(panel_cols, off, B, 0), 0.0))
            a_rows.append(jnp.where(mine, lax.dynamic_slice_in_dim(covariance, off, B, 0), 0.0))
            w_cols.append(jnp.where(mine, lax.dynamic_slice_in_dim(sides, off, B, 1), 0.0))
        rows_buf = jnp.concatenate(
            [jnp.concatenate(s_rows, axis=0), jnp.concatenate(a_rows, axis=0)], axis=1
        )
        w_buf = jnp.concatenate(w_cols, axis=1)
        rows_buf, w_buf = lax.psum((rows_buf, w_buf), "row")
        s_full = rows_buf[:, : K * B]
        a_panel_rows = rows_buf[:, K * B :]
    with jax.named_scope("block_cholesky"):
        chol = jnp.linalg.cholesky(s_full)
    with jax.named_scope("forward_solves"):
        rhs = jnp.concatenate([panel_cols, w_buf], axis=0)
        solved = lax.linalg.triangular_solve(
            chol, rhs, left_side=False, lower=True, transpose_a=True
        )
        factor_rows = solved[:rows_here] * panel_keep(row_tiles, panels)
        z = solved[rows_here:]
        factor_cols_t = (
            lax.linalg.triangular_solve(
                chol, a_panel_rows, left_side=True, lower=True, transpose_a=False
            )
            * panel_keep(col_tiles, panels).T
        )
    with jax.named_scope("complement_update"):
        final_rows = keep_mask(row_tiles, panels)
        final_cols = keep_mask(col_tiles, panels)
        complement = (
            (covariance - dot(factor_rows, factor_cols_t))
            * final_rows[:, None]
            * final_cols[None, :]
        )
    with jax.named_scope("sides_update"):
        new_sides = sides - dot_nt(z, factor_rows)
        for j in range(K):
            off = panels[j] * B - row_start
            placed = lax.dynamic_update_slice_in_dim(
                jnp.zeros_like(new_sides),
                z[:, j * B : (j + 1) * B],
                jnp.clip(off, 0, rows_here - B),
                1,
            )
            new_sides = jnp.where((row_tiles == panels[j])[None, :], placed, new_sides)
    return (complement, factor_rows, new_sides[0], new_sides[1:])


def solution(mesh):
    return jax.shard_map(
        on_device,
        mesh=mesh,
        in_specs=(P("row", "col"), P(), P("row"), P(None, "row")),
        out_specs=(P("row", "col"), P("row", None), P("row"), P(None, "row")),
        check_vma=False,
    )
```

profile of v0, /device:TPU:1, one launch (start us, length us, event | category | flops | bytes accessed | tf_op | source)
XLA Modules:
  0.0 680.8 jit_solution(17626151562019785900)
XLA Ops:
  18.5 89.9 %all-gather.2.cloned.1.call-done = f32[256,8192]{0,1:T(8,128)} async-done(((f32[256,1024]{0,1:T(8,128)}), f32[256,8192]{0,1:T(8,128)}) %all-gather.2.cloned.1.call-update) | async-done | bytes 8388624 | tf_op jit(solution)/shard_map/gather_row_strip/all_gather | solution.py:40
  110.6 10.2 %maximum_maximum_fusion = f32[1024,2048]{0,1:T(8,128)} fusion(f32[256,1024]{0,1:T(8,128)S(1)} %get-tuple-element.46, f32[256,1024]{0,1:T(8,128)S(1)} %copy-done.4, f32[256,1024]{0,1:T(8,128)S(1)} %copy-done.5, f32[256,1024]{0,1:T(8,128)S(1)} %get-tuple-element.45, f32[256,1024]{0,1:T(8,128)S(1)} %broadcast_select_fusion.4, ...), kind=kLoop, calls=%fused_computation.2 | loop fusion | flops 14680064 | bytes 16777216 | tf_op jit(solution)/shard_map/share_panel_rows/concatenate | solution.py:53
  130.0 122.0 %all-reduce.4.cloned.1.call-done = (f32[65,1024]{0,1:T(8,128)}, f32[1024,2048]{0,1:T(8,128)}) async-done(((f32[65,1024]{0,1:T(8,128)}, f32[1024,2048]{0,1:T(8,128)}), (f32[65,1024]{0,1:T(8,128)}, f32[1024,2048]{0,1:T(8,128)})) %all-reduce.4.cloned.1.call-update) | async-done | bytes 8654864 | tf_op jit(solution)/shard_map/share_panel_rows/psum | solution.py:57
  256.7 5.8 copy.50
  269.0 11.7 %cholesky.223 = f32[128,128]{1,0:T(8,128)S(1)} custom-call(f32[128,128]{1,0:T(8,128)S(1)} %cholesky.580), custom_call_target="Cholesky" | custom-call | tf_op jit(solution)/shard_map/block_cholesky/jit(cholesky)/cholesky | solution.py:61
  283.2 9.8 %custom-call.64 = f32[1,128,128]{1,2,0:T(8,128)S(1)} custom-call(f32[1,128,128]{2,1,0:T(8,128)S(1)} %get-tuple-element.123), custom_call_target="InvertDiagBlocksLowerTriangular" | custom-call | tf_op jit(solution)/shard_map/block_cholesky/jit(cholesky)/cholesky | solution.py:61
  297.0 11.9 %cholesky.244 = f32[128,128]{1,0:T(8,128)S(1)} custom-call(f32[128,128]{1,0:T(8,128)S(1)} %cholesky.584), custom_call_target="Cholesky" | custom-call | tf_op jit(solution)/shard_map/block_cholesky/jit(cholesky)/cholesky | solution.py:61
  309.5 9.8 %custom-call.65 = f32[1,128,128]{1,2,0:T(8,128)S(1)} custom-call(f32[1,128,128]{2,1,0:T(8,128)S(1)} %get-tuple-element.120), custom_call_target="InvertDiagBlocksLowerTriangular" | custom-call | tf_op jit(solution)/shard_map/block_cholesky/jit(cholesky)/cholesky | solution.py:61
  322.7 11.7 %cholesky.468 = f32[128,128]{1,0:T(8,128)S(1)} custom-call(f32[128,128]{1,0:T(8,128)S(1)} %cholesky.589), custom_call_target="Cholesky" | custom-call | tf_op jit(solution)/shard_map/block_cholesky/jit(cholesky)/cholesky | solution.py:61
  335.7 9.8 %custom-call.66 = f32[1,128,128]{1,2,0:T(8,128)S(1)} custom-call(f32[1,128,128]{2,1,0:T(8,128)S(1)} %get-tuple-element.117), custom_call_target="InvertDiagBlocksLowerTriangular" | custom-call | tf_op jit(solution)/shard_map/block_cholesky/jit(cholesky)/cholesky | solution.py:61
  349.0 11.9 %cholesky.487 = f32[128,128]{1,0:T(8,128)S(1)} custom-call(f32[128,128]{1,0:T(8,128)S(1)} %cholesky.594), custom_call_target="Cholesky" | custom-call | tf_op jit(solution)/shard_map/block_cholesky/jit(cholesky)/cholesky | solution.py:61
  362.3 9.8 %custom-call.67 = f32[1,128,128]{1,2,0:T(8,128)S(1)} custom-call(f32[1,128,128]{2,1,0:T(8,128)S(1)} %get-tuple-element.114), custom_call_target="InvertDiagBlocksLowerTriangular" | custom-call | tf_op jit(solution)/shard_map/block_cholesky/jit(cholesky)/cholesky | solution.py:61
  375.5 11.7 %cholesky.506 = f32[128,128]{1,0:T(8,128)S(1)} custom-call(f32[128,128]{1,0:T(8,128)S(1)} %cholesky.599), custom_call_target="Cholesky" | custom-call | tf_op jit(solution)/shard_map/block_cholesky/jit(cholesky)/cholesky | solution.py:61
  388.6 10.2 %custom-call.68 = f32[1,128,128]{1,2,0:T(8,128)S(1)} custom-call(f32[1,128,128]{2,1,0:T(8,128)S(1)} %get-tuple-element.111), custom_call_target="InvertDiagBlocksLowerTriangular" | custom-call | tf_op jit(solution)/shard_map/block_cholesky/jit(cholesky)/cholesky | solution.py:61
  402.1 11.7 %cholesky.526 = f32[128,128]{1,0:T(8,128)S(1)} custom-call(f32[128,128]{1,0:T(8,128)S(1)} %cholesky.604), custom_call_target="Cholesky" | custom-call | tf_op jit(solution)/shard_map/block_cholesky/jit(cholesky)/cholesky | solution.py:61
  415.2 9.8 %custom-call.69 = f32[1,128,128]{1,2,0:T(8,128)S(1)} custom-call(f32[1,128,128]{2,1,0:T(8,128)S(1)} %get-tuple-element.108), custom_call_target="InvertDiagBlocksLowerTriangular" | custom-call | tf_op jit(solution)/shard_map/block_cholesky/jit(cholesky)/cholesky | solution.py:61
  428.0 11.9 %cholesky.546 = f32[128,128]{1,0:T(8,128)S(1)} custom-call(f32[128,128]{1,0:T(8,128)S(1)} %cholesky.609), custom_call_target="Cholesky" | custom-call | tf_op jit(solution)/shard_map/block_cholesky/jit(cholesky)/cholesky | solution.py:61
  441.2 9.8 %custom-call.70 = f32[1,128,128]{1,2,0:T(8,128)S(1)} custom-call(f32[1,128,128]{2,1,0:T(8,128)S(1)} %get-tuple-element.105), custom_call_target="InvertDiagBlocksLowerTriangular" | custom-call | tf_op jit(solution)/shard_map/block_cholesky/jit(cholesky)/cholesky | solution.py:61
  453.6 11.7 %cholesky.564 = f32[128,128]{1,0:T(8,128)S(1)} custom-call(f32[128,128]{1,0:T(8,128)S(1)} %convolution_subtract_fusion.19), custom_call_target="Cholesky" | custom-call | tf_op jit(solution)/shard_map/block_cholesky/jit(cholesky)/cholesky | solution.py:61
  477.2 22.5 %while.1 = (s32[]{:T(128)}, f32[1024,1024]{1,0:T(8,128)}, s32[8,2]{0,1:T(2,128)S(1)}, f32[8,128,128]{2,1,0:T(8,128)S(1)}, s32[]{:T(128)}) while((s32[]{:T(128)}, f32[1024,1024]{1,0:T(8,128)}, s32[8,2]{0,1:T(2,128)S(1)}, f32[8,128,128]{2,1,0:T(8,128)S(1)}, s32[]{:T(128)}) %tuple.106), condition=%wide.while_cond, body=%wide.while_body.sunk | while | flops 2 | bytes 131181 | solution.py:64
  499.8 78.8 %custom-call.71 = f32[8,128,128]{1,2,0:T(8,128)S(1)} custom-call(f32[8,128,128]{2,1,0:T(8,128)S(1)} %get-tuple-element.11), custom_call_target="InvertDiagBlocksLowerTriangular" | custom-call | tf_op jit(solution)/shard_map/forward_solves/triangular_solve | solution.py:64
  642.1 6.4 convolution_subtract_fusion.2
  650.4 7.3 %convolution_subtract_fusion.1 = f32[128,1024]{0,1:T(8,128)S(1)} fusion(f32[768,1024]{1,0:T(8,128)} %get-tuple-element.53, f32[1024,2048]{0,1:T(8,128)} %get-tuple-element.33, f32[1024,1024]{1,0:T(8,128)} %get-tuple-element.202), kind=kOutput, calls=%fused_computation.37 | convolution fusion | flops 1208090624 | bytes 4587520 | tf_op jit(solution)/shard_map/forward_solves/triangular_solve | solution.py:70
  659.2 8.5 %convolution_subtract_fusion.3 = f32[128,1024]{0,1:T(8,128)S(1)} fusion(f32[896,1024]{1,0:T(8,128)} %get-tuple-element.49, f32[1024,2048]{0,1:T(8,128)} %get-tuple-element.33, f32[1024,1024]{1,0:T(8,128)} %get-tuple-element.202), kind=kOutput, calls=%fused_computation.41 | convolution fusion | flops 1409417216 | bytes 5177344 | tf_op jit(solution)/shard_map/forward_solves/triangular_solve | solution.py:70
  (198 shorter events, 165.9 us)
Async XLA Ops:
  7.2 101.2 %all-gather.2.cloned.1.call-start = ((), (), s32[]{:S(2)}) async-start(), calls=%async_computation | async-start | bytes 9437184 | tf_op jit(solution)/shard_map/gather_row_strip/all_gather | solution.py:40
  9.7 7.0 %copy-start.1 = (f32[256,1024]{0,1:T(8,128)S(1)}, f32[256,1024]{0,1:T(8,128)}, u32[]{:S(2)}) copy-start(f32[256,1024]{0,1:T(8,128)} %copy.43) | copy-start | bytes 3145732
  9.8 242.2 %all-reduce.4.cloned.1.call-start = ((), (), s32[]{:S(2)}) async-start(), calls=%async_computation.1 | async-start | bytes 17825792 | tf_op jit(solution)/shard_map/share_panel_rows/psum | solution.py:57
  18.5 92.1 %copy-start.4 = (f32[256,1024]{0,1:T(8,128)S(1)}, f32[256,1024]{0,1:T(8,128)}, u32[]{:S(2)}) copy-start(f32[256,1024]{0,1:T(8,128)} %get-tuple-element.47) | copy-start | bytes 3145732
  108.3 2.2 copy-start.5
  109.7 0.7 copy-start.6
  109.7 0.8 copy-start.8
  109.7 0.9 copy-start.10
  267.0 2.0 copy-start
  472.3 106.3 %copy-start.7 = (f32[256,256]{0,1:T(8,128)S(1)}, f32[256,256]{0,1:T(8,128)}, u32[]{:S(2)}) copy-start(f32[256,256]{0,1:T(8,128)} %copy-done.6) | copy-start | bytes 786436
  472.3 106.3 %copy-start.9 = (f32[256,256]{0,1:T(8,128)S(1)}, f32[256,256]{0,1:T(8,128)}, u32[]{:S(2)}) copy-start(f32[256,256]{0,1:T(8,128)} %copy-done.8) | copy-start | bytes 786436
  472.3 106.3 %copy-start.11 = (f32[256,256]{0,1:T(8,128)S(1)}, f32[256,256]{0,1:T(8,128)}, u32[]{:S(2)}) copy-start(f32[256,256]{0,1:T(8,128)} %copy-done.10) | copy-start | bytes 786436
  597.6 13.2 %copy-start.16 = (f32[256]{0:T(256)S(1)}, f32[256]{0:T(256)}, u32[]{:S(2)}) copy-start(f32[256]{0:T(256)} %get-tuple-element.143) | copy-start | bytes 3076
  599.8 11.1 %copy-start.21 = (f32[256]{0:T(256)S(1)}, f32[256]{0:T(256)}, u32[]{:S(2)}) copy-start(f32[256]{0:T(256)} %convert_element_type.57) | copy-start | bytes 3076
  599.8 11.2 %copy-start.22 = (f32[256]{0:T(256)S(1)}, f32[256]{0:T(256)}, u32[]{:S(2)}) copy-start(f32[256]{0:T(256)} %convert_element_type.58) | copy-start | bytes 3076
  603.7 8.9 %copy-start.17 = (pred[256]{0:T(512)(128)(4,1)S(1)}, pred[256]{0:T(512)(128)(4,1)}, u32[]{:S(2)}) copy-start(pred[256]{0:T(512)(128)(4,1)} %get-tuple-element.145) | copy-start | bytes 772
  603.7 8.9 %copy-start.18 = (pred[256]{0:T(512)(128)(4,1)S(1)}, pred[256]{0:T(512)(128)(4,1)}, u32[]{:S(2)}) copy-start(pred[256]{0:T(512)(128)(4,1)} %get-tuple-element.146) | copy-start | bytes 772
  603.7 8.9 %copy-start.19 = (pred[256]{0:T(512)(128)(4,1)S(1)}, pred[256]{0:T(512)(128)(4,1)}, u32[]{:S(2)}) copy-start(pred[256]{0:T(512)(128)(4,1)} %get-tuple-element.144) | copy-start | bytes 772
  603.7 8.9 %copy-start.23 = (pred[256]{0:T(512)(128)(4,1)S(1)}, pred[256]{0:T(512)(128)(4,1)}, u32[]{:S(2)}) copy-start(pred[256]{0:T(512)(128)(4,1)} %broadcast_compare_fusion.3) | copy-start | bytes 772
  612.5 56.2 %copy-start.2 = (f32[256,1024]{1,0:T(8,128)}, f32[256,1024]{1,0:T(8,128)S(1)}, u32[]{:S(2)}) copy-start(f32[256,1024]{1,0:T(8,128)S(1)} %slice_multiply_fusion) | copy-start | bytes 3145732
  650.4 7.3 %copy-start.3 = (f32[1024,1024]{1,0:T(8,128)S(1)}, f32[1024,1024]{1,0:T(8,128)}, u32[]{:S(2)}) copy-start(f32[1024,1024]{1,0:T(8,128)} %get-tuple-element.52) | copy-start | bytes 12582916
  657.7 10.6 %copy-start.15 = (f32[1024]{0:T(1024)S(1)}, f32[1024]{0:T(1024)}, u32[]{:S(2)}) copy-start(f32[1024]{0:T(1024)} %compare_convert_fusion) | copy-start | bytes 12292
  659.2 9.5 %copy-start.12 = (f32[256,1024]{1,0:T(8,128)S(1)}, f32[256,1024]{1,0:T(8,128)}, u32[]{:S(2)}) copy-start(f32[256,1024]{1,0:T(8,128)} %param.4) | copy-start | bytes 3145732
  659.2 9.6 %copy-start.20 = (f32[256]{0:T(256)S(1)}, f32[256]{0:T(256)}, u32[]{:S(2)}) copy-start(f32[256]{0:T(256)} %convert_element_type.62) | copy-start | bytes 3076
  (2 other events, 1.3 us)
Sparse Core Ops, SparseCore 0:
  10.4 97.9 all-gather.1
  121.0 130.9 all-reduce.3
where the time goes:
time: 688 us; the launch traced here: 681 us
  other arithmetic  285 us (41%)
  waiting for transfers between devices  212 us (31%)
  matrix products  108 us (16%)
  local copies, waits for them, and re-layouts  53.2 us (8%)
  between operations  22.7 us (3%)
    another operation x30, other arithmetic, on_device(): chol = jnp.linalg.cholesky(s_full)  172 us
    psum x1, waiting for transfers between devices, on_device(): rows_buf, w_buf = lax.psum((rows_buf, w_buf), 'row')  122 us
    all_gather x1, waiting for transfers between devices, on_device(): strip = lax.all_gather(covariance, 'col', axis=1, tiled=True)  89.9 us
    another operation x3, other arithmetic, on_device(): lax.linalg.triangular_solve(chol, rhs, left_side=False, lower=True, trans...  83.7 us
    another operation x15, matrix products, on_device(): lax.linalg.triangular_solve(chol, a_panel_rows, left_side=True, lower=Tru...  51.8 us
    another operation x15, matrix products, on_device(): lax.linalg.triangular_solve(chol, rhs, left_side=False, lower=True, trans...  25.6 us
    another operation x14, matrix products, on_device(): chol = jnp.linalg.cholesky(s_full)  23.1 us
    another operation x24, local copies, waits for them, and re-layouts  22.4 us
  transfers between devices with their start and end apart: 2, of which 2 were waited for; matrix products, arithmetic and copies ran while one was open for 2% of the time, Pallas kernels for 0%

commit v1 on v0

--- a/solution.py
+++ b/solution.py
@@ -37,7 +37,9 @@
     col_tiles = (col_start + lax.iota(jnp.int32, cols_here)) // B
     sides = jnp.concatenate([observed[None, :], drift_basis], axis=0)
     with jax.named_scope("gather_row_strip"):
-        strip = lax.all_gather(covariance, "col", axis=1, tiled=True)
+        strip = jnp.concatenate(
+            lax.all_to_all(jnp.stack([covariance] * lax.axis_size("col")), "col", 0, 0), axis=1
+        )
         panel_cols = jnp.concatenate(
             [lax.dynamic_slice_in_dim(strip, panels[j] * B, B, 1) for j in range(K)], axis=1
         )

time: 688 us -> 787 us (1.14)
  waiting for transfers between devices: 212 us -> 301 us
  starting transfers between devices: 0.08 us -> 9.18 us
    all_to_all x0 -> x1, waiting for transfers between devices: none -> 181 us  [on_device(): lax.all_to_all(jnp.stack([covariance] * lax.axis_size('col')), 'col', 0, 0)]
    all_gather x1 -> x0, waiting for transfers between devices: 89.9 us -> none  [on_device(): strip = lax.all_gather(covariance, 'col', axis=1, tiled=True)]
    all_to_all x0 -> x1, starting transfers between devices: none -> 9.15 us  [on_device(): lax.all_to_all(jnp.stack([covariance] * lax.axis_size('col')), 'col', 0, 0)]
    another operation x24 -> x25, local copies, waits for them, and re-layouts: 22.4 us -> 27 us
where the time goes in v1:
time: 787 us; the launch traced here: 780 us
  waiting for transfers between devices  301 us (38%)
  other arithmetic  285 us (36%)
  matrix products  108 us (14%)
  local copies, waits for them, and re-layouts  54 us (7%)
  between operations  22.7 us (3%)
  starting transfers between devices  9.18 us (1%)
    all_to_all x1, waiting for transfers between devices, on_device(): lax.all_to_all(jnp.stack([covariance] * lax.axis_size('col')), 'col', 0, 0)  181 us
    another operation x30, other arithmetic, on_device(): chol = jnp.linalg.cholesky(s_full)  172 us
    psum x1, waiting for transfers between devices, on_device(): rows_buf, w_buf = lax.psum((rows_buf, w_buf), 'row')  120 us
    another operation x3, other arithmetic, on_device(): lax.linalg.triangular_solve(chol, rhs, left_side=False, lower=True, trans...  83.7 us
    another operation x15, matrix products, on_device(): lax.linalg.triangular_solve(chol, a_panel_rows, left_side=True, lower=Tru...  51.8 us
    another operation x15, matrix products, on_device(): lax.linalg.triangular_solve(chol, rhs, left_side=False, lower=True, trans...  25.6 us
    another operation x14, matrix products, on_device(): chol = jnp.linalg.cholesky(s_full)  23.1 us
    another operation x24, local copies, waits for them, and re-layouts  23 us
  transfers between devices with their start and end apart: 2, of which 2 were waited for; matrix products, arithmetic and copies ran while one was open for 2% of the time, Pallas kernels for 0%

profile of v1, /device:TPU:1, one launch (start us, length us, event | category | flops | bytes accessed | tf_op | source)
XLA Modules:
  0.0 779.6 jit_solution(10412070366422848344)
XLA Ops:
  12.7 9.1 %all-to-all-start = ((f32[8,256,1024]{1,2,0:T(8,128)}), f32[8,256,1024]{1,2,0:T(8,128)}, u32[]{:S(2)}, u32[]{:S(2)}) async-start(f32[8,256,1024]{1,2,0:T(8,128)} %stack.2), calls=%async_computation | async-start | bytes 16777216 | tf_op jit(solution)/shard_map/gather_row_strip/all_to_all | solution.py:41
  28.0 180.9 %all-to-all-done = f32[8,256,1024]{1,2,0:T(8,128)} async-done(((f32[8,256,1024]{1,2,0:T(8,128)}), f32[8,256,1024]{1,2,0:T(8,128)}, u32[]{:S(2)}, u32[]{:S(2)}) %all-to-all-start) | async-done | bytes 8388640 | tf_op jit(solution)/shard_map/gather_row_strip/all_to_all | solution.py:41
  211.2 10.2 %maximum_maximum_fusion = f32[1024,2048]{0,1:T(8,128)} fusion(f32[256,1024]{0,1:T(8,128)S(1)} %get-tuple-element.46, f32[256,1024]{0,1:T(8,128)S(1)} %copy-done.3, f32[256,1024]{0,1:T(8,128)S(1)} %copy-done.4, f32[256,1024]{0,1:T(8,128)S(1)} %get-tuple-element.45, f32[256,1024]{0,1:T(8,128)S(1)} %broadcast_select_fusion.4, ...), kind=kLoop, calls=%fused_computation.2 | loop fusion | flops 14680064 | bytes 16777216 | tf_op jit(solution)/shard_map/share_panel_rows/concatenate | solution.py:55
  229.9 120.2 %all-reduce.4.cloned.1.call-done = (f32[65,1024]{0,1:T(8,128)}, f32[1024,2048]{0,1:T(8,128)}) async-done(((f32[65,1024]{0,1:T(8,128)}, f32[1024,2048]{0,1:T(8,128)}), (f32[65,1024]{0,1:T(8,128)}, f32[1024,2048]{0,1:T(8,128)})) %all-reduce.4.cloned.1.call-update) | async-done | bytes 8654864 | tf_op jit(solution)/shard_map/share_panel_rows/psum | solution.py:59
  367.1 11.7 %cholesky.223 = f32[128,128]{1,0:T(8,128)S(1)} custom-call(f32[128,128]{1,0:T(8,128)S(1)} %cholesky.580), custom_call_target="Cholesky" | custom-call | tf_op jit(solution)/shard_map/block_cholesky/jit(cholesky)/cholesky | solution.py:63
  381.3 9.8 %custom-call.64 = f32[1,128,128]{1,2,0:T(8,128)S(1)} custom-call(f32[1,128,128]{2,1,0:T(8,128)S(1)} %get-tuple-element.123), custom_call_target="InvertDiagBlocksLowerTriangular" | custom-call | tf_op jit(solution)/shard_map/block_cholesky/jit(cholesky)/cholesky | solution.py:63
  395.1 11.9 %cholesky.244 = f32[128,128]{1,0:T(8,128)S(1)} custom-call(f32[128,128]{1,0:T(8,128)S(1)} %cholesky.584), custom_call_target="Cholesky" | custom-call | tf_op jit(solution)/shard_map/block_cholesky/jit(cholesky)/cholesky | solution.py:63
  407.6 9.8 %custom-call.65 = f32[1,128,128]{1,2,0:T(8,128)S(1)} custom-call(f32[1,128,128]{2,1,0:T(8,128)S(1)} %get-tuple-element.120), custom_call_target="InvertDiagBlocksLowerTriangular" | custom-call | tf_op jit(solution)/shard_map/block_cholesky/jit(cholesky)/cholesky | solution.py:63
  420.8 11.7 %cholesky.468 = f32[128,128]{1,0:T(8,128)S(1)} custom-call(f32[128,128]{1,0:T(8,128)S(1)} %cholesky.589), custom_call_target="Cholesky" | custom-call | tf_op jit(solution)/shard_map/block_cholesky/jit(cholesky)/cholesky | solution.py:63
  433.8 9.8 %custom-call.66 = f32[1,128,128]{1,2,0:T(8,128)S(1)} custom-call(f32[1,128,128]{2,1,0:T(8,128)S(1)} %get-tuple-element.117), custom_call_target="InvertDiagBlocksLowerTriangular" | custom-call | tf_op jit(solution)/shard_map/block_cholesky/jit(cholesky)/cholesky | solution.py:63
  447.1 11.9 %cholesky.487 = f32[128,128]{1,0:T(8,128)S(1)} custom-call(f32[128,128]{1,0:T(8,128)S(1)} %cholesky.594), custom_call_target="Cholesky" | custom-call | tf_op jit(solution)/shard_map/block_cholesky/jit(cholesky)/cholesky | solution.py:63
  460.4 9.8 %custom-call.67 = f32[1,128,128]{1,2,0:T(8,128)S(1)} custom-call(f32[1,128,128]{2,1,0:T(8,128)S(1)} %get-tuple-element.114), custom_call_target="InvertDiagBlocksLowerTriangular" | custom-call | tf_op jit(solution)/shard_map/block_cholesky/jit(cholesky)/cholesky | solution.py:63
  473.7 11.7 %cholesky.506 = f32[128,128]{1,0:T(8,128)S(1)} custom-call(f32[128,128]{1,0:T(8,128)S(1)} %cholesky.599), custom_call_target="Cholesky" | custom-call | tf_op jit(solution)/shard_map/block_cholesky/jit(cholesky)/cholesky | solution.py:63
  486.8 10.2 %custom-call.68 = f32[1,128,128]{1,2,0:T(8,128)S(1)} custom-call(f32[1,128,128]{2,1,0:T(8,128)S(1)} %get-tuple-element.111), custom_call_target="InvertDiagBlocksLowerTriangular" | custom-call | tf_op jit(solution)/shard_map/block_cholesky/jit(cholesky)/cholesky | solution.py:63
  500.3 11.7 %cholesky.526 = f32[128,128]{1,0:T(8,128)S(1)} custom-call(f32[128,128]{1,0:T(8,128)S(1)} %cholesky.604), custom_call_target="Cholesky" | custom-call | tf_op jit(solution)/shard_map/block_cholesky/jit(cholesky)/cholesky | solution.py:63
  513.3 9.8 %custom-call.69 = f32[1,128,128]{1,2,0:T(8,128)S(1)} custom-call(f32[1,128,128]{2,1,0:T(8,128)S(1)} %get-tuple-element.108), custom_call_target="InvertDiagBlocksLowerTriangular" | custom-call | tf_op jit(solution)/shard_map/block_cholesky/jit(cholesky)/cholesky | solution.py:63
  526.1 11.9 %cholesky.546 = f32[128,128]{1,0:T(8,128)S(1)} custom-call(f32[128,128]{1,0:T(8,128)S(1)} %cholesky.609), custom_call_target="Cholesky" | custom-call | tf_op jit(solution)/shard_map/block_cholesky/jit(cholesky)/cholesky | solution.py:63
  539.3 9.8 %custom-call.70 = f32[1,128,128]{1,2,0:T(8,128)S(1)} custom-call(f32[1,128,128]{2,1,0:T(8,128)S(1)} %get-tuple-element.105), custom_call_target="InvertDiagBlocksLowerTriangular" | custom-call | tf_op jit(solution)/shard_map/block_cholesky/jit(cholesky)/cholesky | solution.py:63
  551.8 11.7 %cholesky.564 = f32[128,128]{1,0:T(8,128)S(1)} custom-call(f32[128,128]{1,0:T(8,128)S(1)} %convolution_subtract_fusion.19), custom_call_target="Cholesky" | custom-call | tf_op jit(solution)/shard_map/block_cholesky/jit(cholesky)/cholesky | solution.py:63
  575.4 23.2 %while.1 = (s32[]{:T(128)}, f32[1024,1024]{1,0:T(8,128)}, s32[8,2]{0,1:T(2,128)S(1)}, f32[8,128,128]{2,1,0:T(8,128)S(1)}, s32[]{:T(128)}) while((s32[]{:T(128)}, f32[1024,1024]{1,0:T(8,128)}, s32[8,2]{0,1:T(2,128)S(1)}, f32[8,128,128]{2,1,0:T(8,128)S(1)}, s32[]{:T(128)}) %tuple.106), condition=%wide.while_cond, body=%wide.while_body.sunk | while | flops 2 | bytes 131181 | solution.py:66
  598.6 78.8 %custom-call.71 = f32[8,128,128]{1,2,0:T(8,128)S(1)} custom-call(f32[8,128,128]{2,1,0:T(8,128)S(1)} %get-tuple-element.11), custom_call_target="InvertDiagBlocksLowerTriangular" | custom-call | tf_op jit(solution)/shard_map/forward_solves/triangular_solve | solution.py:66
  740.9 6.4 convolution_subtract_fusion.2
  749.2 7.3 convolution_subtract_fusion.1
  758.0 8.5 %convolution_subtract_fusion.3 = f32[128,1024]{0,1:T(8,128)S(1)} fusion(f32[896,1024]{1,0:T(8,128)} %get-tuple-element.49, f32[1024,2048]{0,1:T(8,128)} %get-tuple-element.33, f32[1024,1024]{1,0:T(8,128)} %get-tuple-element.203), kind=kOutput, calls=%fused_computation.41 | convolution fusion | flops 1409417216 | bytes 5177344 | tf_op jit(solution)/shard_map/forward_solves/triangular_solve | solution.py:72
  (200 shorter events, 172.2 us)
Async XLA Ops:
  12.7 9.2 %copy-start.14 = (s32[4]{0:T(128)S(1)}, s32[4]{0:T(128)}, u32[]{:S(2)}) copy-start(s32[4]{0:T(128)} %param.5) | copy-start | bytes 52
  12.7 12.4 %copy-start.20 = (f32[256]{0:T(256)S(1)}, f32[256]{0:T(256)}, u32[]{:S(2)}) copy-start(f32[256]{0:T(256)} %param.6) | copy-start | bytes 3076
  12.7 12.5 %copy-start.13 = (f32[64,256]{1,0:T(8,128)S(1)}, f32[64,256]{1,0:T(8,128)}, u32[]{:S(2)}) copy-start(f32[64,256]{1,0:T(8,128)} %param.7) | copy-start | bytes 196612
  12.7 196.2 %all-to-all-start = ((f32[8,256,1024]{1,2,0:T(8,128)}), f32[8,256,1024]{1,2,0:T(8,128)}, u32[]{:S(2)}, u32[]{:S(2)}) async-start(f32[8,256,1024]{1,2,0:T(8,128)} %stack.2), calls=%async_computation | async-start | bytes 16777216 | tf_op jit(solution)/shard_map/gather_row_strip/all_to_all | solution.py:41
  21.8 328.3 %all-reduce.4.cloned.1.call-start = ((), (), s32[]{:S(2)}) async-start(), calls=%async_computation.1 | async-start | bytes 17825792 | tf_op jit(solution)/shard_map/share_panel_rows/psum | solution.py:59
  208.9 2.3 copy-start.3
  208.9 2.3 copy-start.4
  210.3 0.9 copy-start.9
  365.1 2.0 copy-start
  570.5 107.0 %copy-start.6 = (f32[256,256]{0,1:T(8,128)S(1)}, f32[256,256]{0,1:T(8,128)}, u32[]{:S(2)}) copy-start(f32[256,256]{0,1:T(8,128)} %copy-done.5) | copy-start | bytes 786436
  570.5 107.0 %copy-start.8 = (f32[256,256]{0,1:T(8,128)S(1)}, f32[256,256]{0,1:T(8,128)}, u32[]{:S(2)}) copy-start(f32[256,256]{0,1:T(8,128)} %copy-done.7) | copy-start | bytes 786436
  570.5 107.0 %copy-start.10 = (f32[256,256]{0,1:T(8,128)S(1)}, f32[256,256]{0,1:T(8,128)}, u32[]{:S(2)}) copy-start(f32[256,256]{0,1:T(8,128)} %copy-done.9) | copy-start | bytes 786436
  696.4 13.2 %copy-start.16 = (f32[256]{0:T(256)S(1)}, f32[256]{0:T(256)}, u32[]{:S(2)}) copy-start(f32[256]{0:T(256)} %get-tuple-element.143) | copy-start | bytes 3076
  698.7 11.1 %copy-start.22 = (f32[256]{0:T(256)S(1)}, f32[256]{0:T(256)}, u32[]{:S(2)}) copy-start(f32[256]{0:T(256)} %convert_element_type.57) | copy-start | bytes 3076
  698.7 11.2 %copy-start.23 = (f32[256]{0:T(256)S(1)}, f32[256]{0:T(256)}, u32[]{:S(2)}) copy-start(f32[256]{0:T(256)} %convert_element_type.58) | copy-start | bytes 3076
  702.5 8.9 %copy-start.17 = (pred[256]{0:T(512)(128)(4,1)S(1)}, pred[256]{0:T(512)(128)(4,1)}, u32[]{:S(2)}) copy-start(pred[256]{0:T(512)(128)(4,1)} %get-tuple-element.145) | copy-start | bytes 772
  702.5 8.9 %copy-start.18 = (pred[256]{0:T(512)(128)(4,1)S(1)}, pred[256]{0:T(512)(128)(4,1)}, u32[]{:S(2)}) copy-start(pred[256]{0:T(512)(128)(4,1)} %get-tuple-element.146) | copy-start | bytes 772
  702.5 8.9 %copy-start.19 = (pred[256]{0:T(512)(128)(4,1)S(1)}, pred[256]{0:T(512)(128)(4,1)}, u32[]{:S(2)}) copy-start(pred[256]{0:T(512)(128)(4,1)} %get-tuple-element.144) | copy-start | bytes 772
  702.5 8.9 %copy-start.24 = (pred[256]{0:T(512)(128)(4,1)S(1)}, pred[256]{0:T(512)(128)(4,1)}, u32[]{:S(2)}) copy-start(pred[256]{0:T(512)(128)(4,1)} %broadcast_compare_fusion.3) | copy-start | bytes 772
  711.4 56.2 %copy-start.1 = (f32[256,1024]{1,0:T(8,128)}, f32[256,1024]{1,0:T(8,128)S(1)}, u32[]{:S(2)}) copy-start(f32[256,1024]{1,0:T(8,128)S(1)} %slice_multiply_fusion) | copy-start | bytes 3145732
  749.2 7.3 copy-start.2
  756.5 10.6 %copy-start.15 = (f32[1024]{0:T(1024)S(1)}, f32[1024]{0:T(1024)}, u32[]{:S(2)}) copy-start(f32[1024]{0:T(1024)} %compare_convert_fusion) | copy-start | bytes 12292
  758.0 9.5 %copy-start.11 = (f32[256,1024]{1,0:T(8,128)S(1)}, f32[256,1024]{1,0:T(8,128)}, u32[]{:S(2)}) copy-start(f32[256,1024]{1,0:T(8,128)} %param.4) | copy-start | bytes 3145732
  758.0 9.6 %copy-start.21 = (f32[256]{0:T(256)S(1)}, f32[256]{0:T(256)}, u32[]{:S(2)}) copy-start(f32[256]{0:T(256)} %convert_element_type.62) | copy-start | bytes 3076
  (3 other events, 2.2 us)
Sparse Core Ops, SparseCore 0:
  221.6 128.4 all-reduce.3
